TPU v7x, 32 devices: a whole 2x2x4 slice. The times are simulated.
32 devices in a mesh: dp: 8 (over z, core), leaf: 4 (over y, x).
Axes of the slice: x: 2, y: 2, z: 4, core: 2. Of those that a mesh axis runs over, the one named last changes fastest.
Arguments:
- features: bfloat16 [51200, 384], P(('dp', 'leaf')), may hold values from -6 to 6
- head_weight: bfloat16 [384, 1536], replicated, may hold values from -0.3125 to 0.3125
- gain: float32 [1536], replicated, may hold values from 0.5 to 1.5
- shift: float32 [1536], replicated, may hold values from -3 to 3
- node_weights: bfloat16 [4096, 1536], P('leaf'), may hold values from -0.15625 to 0.15625
- subtree_map: int32 [64], replicated, may hold values from 0 to 63, each once
- node_ids: int32 [512, 64], P('dp'), may hold values from -1 to 4095, as said below
Outputs:
- head_grad: float32 [384, 1536], P(None, 'dp')
- gain_grad: float32 [1536], P('dp')
- shift_grad: float32 [1536], P('dp')
- node_grad: float32 [4096, 1536], P('leaf', 'dp')
Inputs may be any that keep to these rules, and one draw needn't show every extreme that they name: `node_ids`: each image has 1 to 16 positive ids, all in one subtree, in its first columns, then -1; and 1 to 48 hard-negative ids in another subtree from column 16 on, then -1. Ids of one image are distinct. The first image has full counts.
All inputs are finite; a program needn't handle non-finite values.
Results may differ from a plain program's by a relative error of at most 0.0036.
Values may be sent and summed in bfloat16 or wider, within the bound.
No kernel may reach another device: no remote copies, remote signals or barrier semaphores. Data moves between devices by JAX's collectives and lax.ppermute only.
A program may use at most 128 MiB of HBM per device.

v0:
```python
import jax
import jax.numpy as jnp
from jax import lax
from jax.sharding import PartitionSpec as P

P_SIZE = 100
SUB_SIZE = 64
KPOS = 16


def slot_table(slot_rows, owned_rows, values_rows, slots_dev):
    column = jnp.arange(slots_dev, dtype=jnp.int32)[None, None, :]
    match = (slot_rows[:, :, None] == column) & owned_rows[:, :, None]
    return jnp.sum(jnp.where(match, values_rows[:, :, None], 0.0), axis=1)


def shards(features, head_weight, gain, shift, node_weights, subtree_map, node_ids):
    images_here = features.shape[0] // P_SIZE
    width = head_weight.shape[1]
    linear_scores = jnp.dot(features, head_weight, preferred_element_type=jnp.float32)
    shifted = gain * linear_scores + shift
    sig = jax.nn.sigmoid(shifted)
    active = shifted * sig
    embedded = jnp.mean(active.reshape(images_here, P_SIZE, width), axis=1).astype(jnp.bfloat16)
    grouped = lax.all_gather(embedded, "leaf", axis=0, tiled=True)
    slots_dev = node_weights.shape[0]
    valid_pair = node_ids >= 0
    safe_ids = jnp.where(valid_pair, node_ids, 0)
    subtree = safe_ids // SUB_SIZE
    matches = (
        subtree[:, :, None] == jnp.arange(subtree_map.shape[0], dtype=jnp.int32)[None, None, :]
    )
    placed = jnp.sum(jnp.where(matches, subtree_map[None, None, :], 0), axis=2)
    slot_row = placed * SUB_SIZE + safe_ids % SUB_SIZE
    owned = valid_pair & (slot_row // slots_dev == lax.axis_index("leaf"))
    local_slot = jnp.where(owned, slot_row % slots_dev, 0)
    scores = lax.dot_general(
        grouped, node_weights, (((1,), (1,)), ((), ())), preferred_element_type=jnp.float32
    )
    target = (jnp.arange(node_ids.shape[1]) < KPOS).astype(jnp.float32)
    hit_count = slot_table(local_slot, owned, jnp.ones(local_slot.shape, jnp.float32), slots_dev)
    positive = slot_table(
        local_slot, owned, jnp.broadcast_to(target[None, :], local_slot.shape), slots_dev
    )
    table = jnp.where(hit_count > 0.5, jax.nn.sigmoid(scores) - positive, 0.0).astype(jnp.bfloat16)
    grad_part = jnp.dot(table, node_weights, preferred_element_type=jnp.float32)
    emb_grad = lax.psum_scatter(grad_part, "leaf", scatter_dimension=0, tiled=True)
    column_ids = jnp.arange(slots_dev, dtype=jnp.int32)[None, None, :]
    pick = (local_slot[:, :, None] == column_ids) & owned[:, :, None]
    coef = jnp.sum(jnp.where(pick, table.astype(jnp.float32)[:, None, :], 0.0), axis=2).astype(
        jnp.bfloat16
    )
    columns = lax.all_to_all(grouped, "dp", split_axis=1, concat_axis=0, tiled=True)
    all_coef = lax.all_gather(coef, "dp", axis=0, tiled=True)
    all_slot = lax.all_gather(local_slot, "dp", axis=0, tiled=True)
    every_pair = jnp.ones(all_slot.shape, jnp.bool_)
    all_table = slot_table(all_slot, every_pair, all_coef.astype(jnp.float32), slots_dev).astype(
        jnp.bfloat16
    )
    node_grad = lax.dot_general(
        all_table, columns, (((0,), (0,)), ((), ())), preferred_element_type=jnp.float32
    )
    slope = (sig * (1.0 + shifted * (1.0 - sig))).reshape(images_here, P_SIZE, width)
    pixel_gradient = ((emb_grad / P_SIZE)[:, None, :] * slope).reshape(images_here * P_SIZE, width)
    lin_grad = (pixel_gradient * gain).astype(jnp.bfloat16)
    head_term = lax.dot_general(
        features, lin_grad, (((0,), (0,)), ((), ())), preferred_element_type=jnp.float32
    )
    gain_term = jnp.sum(pixel_gradient * linear_scores, axis=0)
    shift_term = jnp.sum(pixel_gradient, axis=0)
    split_sums = (
        lax.psum_scatter(head_term, "dp", scatter_dimension=1, tiled=True),
        lax.psum_scatter(gain_term, "dp", scatter_dimension=0, tiled=True),
        lax.psum_scatter(shift_term, "dp", scatter_dimension=0, tiled=True),
    )
    head_grad, gain_grad, shift_grad = lax.psum(
        (split_sums[0], split_sums[1], split_sums[2]), "leaf"
    )
    return (head_grad, gain_grad, shift_grad, node_grad)


def solution(mesh):
    in_specs = (P(("dp", "leaf"), None), P(), P(), P(), P("leaf", None), P(), P("dp", None))
    out_specs = (P(None, "dp"), P("dp"), P("dp"), P("leaf", "dp"))
    return jax.shard_map(shards, mesh=mesh, in_specs=in_specs, out_specs=out_specs, check_vma=False)
```

profile of v0, /device:TPU:0, one launch (start us, length us, event | category | flops | bytes accessed | tf_op | source)
XLA Modules:
  0.0 237.6 jit_solution(990321862324019750)
XLA Ops:
  7.2 0.0 copy-start
  7.2 0.0 reduce-scatter.3.cloned.1.call-start
  7.2 0.9 add_select_fusion.3
  8.2 11.9 %fusion.1 = (f32[1600,1536]{1,0:T(8,128)}, f32[1600,1536]{1,0:T(8,128)}) fusion(f32[1536]{0:T(1024)} %param.10, f32[1536]{0:T(1024)} %param.9, bf16[1600,384]{1,0:T(8,128)(2,1)} %param.7, bf16[384,1536]{1,0:T(8,128)(2,1)} %param.8), kind=kOutput, calls=%fused_computation.11 | convolution fusion | flops 1902182400 | bytes 22081536 | tf_op jit(solution)/shard_map/dot_general | solution.py:20
  20.1 10.0 %reshape.27 = f32[16,100,1536]{2,1,0:T(8,128)} reshape(f32[1600,1536]{1,0:T(8,128)} %get-tuple-element.15) | data formatting | bytes 19660800 | tf_op jit(solution)/shard_map/reshape | solution.py:24
  30.1 0.0 copy-start.4
  30.1 0.0 copy-start.1
  30.1 5.3 %reduce_sum.74 = f32[16,1536]{1,0:T(8,128)S(1)} reduce(f32[16,100,1536]{2,1,0:T(8,128)} %reshape.27, f32[]{:T(128)} %constant.65.clone.1), dimensions={1}, to_apply=%region_2.3 | reduce | flops 2433024 | bytes 9928708 | tf_op jit(solution)/shard_map/reduce_sum | solution.py:24
  35.5 10.2 %all_gather.9 = bf16[64,1536]{1,0:T(8,128)(2,1)S(1)} all-gather(bf16[16,1536]{1,0:T(8,128)(2,1)S(1)} %multiply_convert_fusion.4), channel_id=1, replica_groups=mesh['dp'=8,'leaf'=4] {'leaf'}, dimensions={0}, use_global_device_ids=true | all-gather | bytes 245760 | tf_op jit(solution)/shard_map/all_gather | solution.py:25
  45.6 0.0 copy-done.4
  45.6 1.8 select_reduce_fusion.4
  47.5 0.0 copy-done.1
  47.5 0.1 fusion.15
  47.6 9.4 %select_reduce_fusion.3 = (f32[64,1024]{1,0:T(8,128)S(1)}, f32[64,1024]{1,0:T(8,128)S(1)}) fusion(s32[64,64]{1,0:T(8,128)S(1)} %get-tuple-element.13, pred[64,64]{1,0:T(8,128)(4,1)S(1)} %get-tuple-element.14, f32[64]{0:T(128)S(1)} %compare_convert_fusion), kind=kLoop, calls=%fused_computation.4 | loop fusion | flops 25034752 | bytes 545024 | tf_op jit(solution)/shard_map/reduce_sum | solution.py:14
  56.9 0.0 copy-done
  56.9 1.8 fusion.21
  58.7 1.4 fusion.22
  60.1 0.0 reduce-scatter.3.cloned.1.call-update
  60.2 0.2 reduce-scatter.5.cloned.1.call-start
  60.4 24.7 %reduce-scatter.3.cloned.1.call-done = f32[16,1536]{1,0:T(8,128)} async-done(((f32[64,1536]{1,0:T(8,128)}), f32[16,1536]{1,0:T(8,128)}) %reduce-scatter.3.cloned.1.call-update) | async-done | bytes 98320 | tf_op jit(solution)/shard_map/reduce_scatter | solution.py:47
  85.1 0.9 broadcast_multiply_fusion
  86.0 5.2 %mul.45 = f32[16,100,1536]{2,1,0:T(8,128)} broadcast(f32[16,1536]{1,0:T(8,128)S(1)} %broadcast_multiply_fusion), dimensions={0,2} | broadcast | bytes 9928704 | tf_op jit(solution)/shard_map/mul | solution.py:64
  91.2 10.0 %mul.46 = f32[1600,1536]{1,0:T(8,128)} reshape(f32[16,100,1536]{2,1,0:T(8,128)} %mul.45) | data formatting | bytes 19660800 | tf_op jit(solution)/shard_map/mul | solution.py:64
  101.2 0.0 copy-done.2
  101.2 0.0 copy-done.3
  101.2 9.0 %fusion.20 = (f32[1536]{0:T(1024)S(1)}, f32[1536]{0:T(1024)S(1)}, f32[1600,1536]{1,0:T(8,128)S(1)}) fusion(f32[1600,1536]{1,0:T(8,128)} %get-tuple-element.16, f32[1600,1536]{1,0:T(8,128)} %mul.46, f32[1536]{0:T(1024)S(1)} %copy-done.2, f32[1536]{0:T(1024)S(1)} %copy-done.3), kind=kLoop, calls=%fused_computation.52 | loop fusion | flops 31945728 | bytes 29515776 | tf_op jit(solution)/shard_map/reduce_sum | solution.py:70
  110.2 0.0 copy-done.5
  110.3 0.0 copy-start.6
  110.3 4.5 %fusion.4 = f32[384,1536]{0,1:T(8,128)} fusion(bf16[1600,384]{1,0:T(8,128)(2,1)S(1)} %copy-done.5, f32[1600,1536]{1,0:T(8,128)S(1)} %get-tuple-element.12, f32[1536]{0:T(1024)S(1)} %copy-done.3), kind=kOutput, calls=%fused_computation.15 | convolution fusion | flops 1892352000 | bytes 13424640 | tf_op jit(solution)/shard_map/dot_general | solution.py:66
  114.7 0.0 reduce-scatter.5.cloned.1.call-update
  114.8 0.9 all_to_all.14
  115.7 1.7 copy.13
  117.4 4.6 %all-to-all-start = ((bf16[64,8,192]{2,0,1:T(8,128)(2,1)}), bf16[64,8,192]{2,0,1:T(8,128)(2,1)}, u32[]{:S(2)}, u32[]{:S(2)}) async-start(bf16[64,8,192]{2,0,1:T(8,128)(2,1)} %copy.13), calls=%async_computation.2 | async-start | bytes 524288 | tf_op jit(solution)/shard_map/all_to_all | solution.py:53
  122.0 0.0 all-reduce.6.cloned.1.call-start
  122.1 5.3 %select_reduce_fusion.1 = bf16[64,64]{1,0:T(8,128)(2,1)S(1)} fusion(f32[64,1024]{1,0:T(8,128)} %get-tuple-element.17, s32[64,64]{1,0:T(8,128)S(1)} %get-tuple-element.13, pred[64,64]{1,0:T(8,128)(4,1)S(1)} %get-tuple-element.14), kind=kLoop, calls=%fused_computation.2 | loop fusion | flops 16773120 | bytes 290816 | tf_op jit(solution)/shard_map/reduce_sum | solution.py:50
  127.4 16.8 %all_gather.11 = bf16[512,64]{1,0:T(8,128)(2,1)S(1)} all-gather(bf16[64,64]{1,0:T(8,128)(2,1)S(1)} %select_reduce_fusion.1), channel_id=1, replica_groups=mesh['dp'=8,'leaf'=4] {'dp'}, dimensions={0}, use_global_device_ids=true | all-gather | bytes 73728 | tf_op jit(solution)/shard_map/all_gather | solution.py:54
  144.3 15.8 %all_gather.10 = s32[512,64]{1,0:T(8,128)} all-gather(s32[64,64]{1,0:T(8,128)S(1)} %get-tuple-element.13), channel_id=1, replica_groups=mesh['dp'=8,'leaf'=4] {'dp'}, dimensions={0}, use_global_device_ids=true | all-gather | bytes 147456 | tf_op jit(solution)/shard_map/all_gather | solution.py:55
  160.1 0.0 all-reduce.6.cloned.1.call-update
  160.1 28.2 %select_reduce_fusion = bf16[512,1024]{1,0:T(8,128)(2,1)} fusion(f32[512,64]{1,0:T(8,128)S(1)} %convert_element_type.30, s32[512,64]{1,0:T(8,128)} %all_gather.10), kind=kLoop, calls=%fused_computation | loop fusion | flops 100139008 | bytes 1310720 | tf_op jit(solution)/shard_map/reduce_sum | solution.py:14
  188.3 0.0 copy-done.6
  188.3 0.6 dynamic-slice
  189.6 0.0 all-to-all-done
  189.6 2.6 %fusion.23 = f32[1024,192]{0,1:T(8,128)} fusion(bf16[512,1024]{1,0:T(8,128)(2,1)} %select_reduce_fusion, bf16[512,192]{1,0:T(8,128)(2,1)} %bitcast.2), kind=kOutput, calls=%fused_computation.55 | convolution fusion | flops 201326592 | bytes 2031616 | tf_op jit(solution)/shard_map/dot_general | solution.py:60
  192.1 27.6 %all-reduce.2 = (f32[1536]{0:T(1024)S(1)}, f32[1536]{0:T(1024)S(1)}) all-reduce(f32[1536]{0:T(1024)S(1)} %get-tuple-element.5, f32[1536]{0:T(1024)S(1)} %get-tuple-element.4), channel_id=4, replica_groups=mesh['dp'=8,'leaf'=4] {'dp'}, use_global_device_ids=true, to_apply=%region_8.9.clone | all-reduce | flops 3072 | bytes 24576
  219.8 0.1 dynamic-slice.1
  219.8 0.1 dynamic-slice.3
  219.9 9.4 %all-reduce.3 = (f32[192]{0:T(256)}, f32[192]{0:T(256)}) all-reduce(f32[192]{0:T(256)S(1)} %dynamic-slice.1, f32[192]{0:T(256)S(1)} %dynamic-slice.3), channel_id=1, replica_groups=mesh['dp'=8,'leaf'=4] {'leaf'}, use_global_device_ids=true, to_apply=%region_9.10 | all-reduce | flops 384 | bytes 3072 | tf_op jit(solution)/shard_map/psum | solution.py:76
  229.4 1.7 copy.15
  (8 shorter events, 0.0 us)
Async XLA Ops:
  7.2 49.8 %copy-start = (bf16[1024,1536]{1,0:T(8,128)(2,1)S(1)}, bf16[1024,1536]{1,0:T(8,128)(2,1)}, u32[]{:S(2)}) copy-start(bf16[1024,1536]{1,0:T(8,128)(2,1)} %param.11) | copy-start | bytes 9437188
  7.2 77.9 %reduce-scatter.3.cloned.1.call-start = ((), (), s32[]{:S(2)}) async-start(), calls=%async_computation.3 | async-start | bytes 491520 | tf_op jit(solution)/shard_map/reduce_scatter | solution.py:47
  30.1 15.5 %copy-start.4 = (s32[64]{0:T(128)S(1)}, s32[64]{0:T(128)}, u32[]{:S(2)}) copy-start(s32[64]{0:T(128)} %param.12) | copy-start | bytes 772
  30.1 17.3 %copy-start.1 = (s32[64,64]{1,0:T(8,128)S(1)}, s32[64,64]{1,0:T(8,128)}, u32[]{:S(2)}) copy-start(s32[64,64]{1,0:T(8,128)} %param.13) | copy-start | bytes 49156
  60.2 99.9 %reduce-scatter.5.cloned.1.call-start = ((), (), s32[]{:S(2)}) async-start(), calls=%async_computation.4 | async-start | bytes 2654208 | tf_op jit(solution)/shard_map/reduce_scatter | solution.py:72
  91.1 10.1 %copy-start.2 = (f32[1536]{0:T(1024)S(1)}, f32[1536]{0:T(1024)}, u32[]{:S(2)}) copy-start(f32[1536]{0:T(1024)} %param.10) | copy-start | bytes 18436
  91.2 10.1 %copy-start.3 = (f32[1536]{0:T(1024)S(1)}, f32[1536]{0:T(1024)}, u32[]{:S(2)}) copy-start(f32[1536]{0:T(1024)} %param.9) | copy-start | bytes 18436
  101.2 9.0 %copy-start.5 = (bf16[1600,384]{1,0:T(8,128)(2,1)S(1)}, bf16[1600,384]{1,0:T(8,128)(2,1)}, u32[]{:S(2)}) copy-start(bf16[1600,384]{1,0:T(8,128)(2,1)} %param.7) | copy-start | bytes 3686404
  110.3 78.1 %copy-start.6 = (u32[32]{0:T(128)S(1)}, u32[32]{0:T(128)}, u32[]{:S(2)}) copy-start(u32[32]{0:T(128)} %constant.71) | copy-start | bytes 388
  117.4 72.2 %all-to-all-start = ((bf16[64,8,192]{2,0,1:T(8,128)(2,1)}), bf16[64,8,192]{2,0,1:T(8,128)(2,1)}, u32[]{:S(2)}, u32[]{:S(2)}) async-start(bf16[64,8,192]{2,0,1:T(8,128)(2,1)} %copy.13), calls=%async_computation.2 | async-start | bytes 524288 | tf_op jit(solution)/shard_map/all_to_all | solution.py:53
  122.0 107.4 %all-reduce.6.cloned.1.call-start = ((), (), s32[]{:S(2)}) async-start(), calls=%async_computation.5 | async-start | bytes 589824 | tf_op jit(solution)/shard_map/psum | solution.py:76
Sparse Core Ops, SparseCore 0:
  60.3 24.7 reduce-scatter.2
  114.9 41.0 reduce-scatter.4
  160.2 41.8 all-reduce.5
where the time goes:
time: 239 us; the launch traced here: 238 us
  blocking collectives  79.9 us (33%)
  other arithmetic  61 us (26%)
  local copies, waits for them, and re-layouts  30.4 us (13%)
  waiting for transfers between devices  24.7 us (10%)
  matrix products  22.2 us (9%)
  between operations  14.5 us (6%)
  starting transfers between devices  4.89 us (2%)
    reduce_sum x2, other arithmetic, slot_table(): return jnp.sum(jnp.where(match, values_rows[:, :, None], 0.0), axis=1)  37.6 us
    unnamed x1, blocking collectives  27.6 us
    reduce_scatter x1, waiting for transfers between devices, shards(): lax.psum_scatter(grad_part, 'leaf', scatter_dimension=0, tiled=True)  24.7 us
    all_gather x1, blocking collectives, shards(): all_coef = lax.all_gather(coef, 'dp', axis=0, tiled=True)  16.8 us
    all_gather x1, blocking collectives, shards(): all_slot = lax.all_gather(local_slot, 'dp', axis=0, tiled=True)  15.8 us
    mul x2, local copies, waits for them, and re-layouts, shards(): (emb_grad / P_SIZE)[:, None, :] * slope  15.2 us
    dot_general x1, matrix products, shards(): jnp.dot(features, head_weight, preferred_element_type=jnp.float32)  11.9 us
    all_gather x1, blocking collectives, shards(): grouped = lax.all_gather(embedded, 'leaf', axis=0, tiled=True)  10.2 us
  transfers between devices with their start and end apart: 4, of which 1 were waited for; matrix products, arithmetic and copies ran while one was open for 16% of the time, Pallas kernels for 0%

commit v1 on v0

--- a/solution.py
+++ b/solution.py
@@ -6,6 +6,16 @@
 P_SIZE = 100
 SUB_SIZE = 64
 KPOS = 16
+
+
+def around_the_ring(x, name, dim):
+    n_dev = lax.axis_size(name)
+    block, blocks = (x, [x])
+    for _ in range(n_dev - 1):
+        block = lax.ppermute(block, name, [(i, (i + 1) % n_dev) for i in range(n_dev)])
+        blocks.insert(0, block)
+    merged = jnp.concatenate(blocks, axis=dim)
+    return jnp.roll(merged, (lax.axis_index(name) + 1) * x.shape[dim], axis=dim)
 
 
 def slot_table(slot_rows, owned_rows, values_rows, slots_dev):
@@ -51,7 +61,7 @@
         jnp.bfloat16
     )
     columns = lax.all_to_all(grouped, "dp", split_axis=1, concat_axis=0, tiled=True)
-    all_coef = lax.all_gather(coef, "dp", axis=0, tiled=True)
+    all_coef = around_the_ring(coef, "dp", 0)
     all_slot = lax.all_gather(local_slot, "dp", axis=0, tiled=True)
     every_pair = jnp.ones(all_slot.shape, jnp.bool_)
     all_table = slot_table(all_slot, every_pair, all_coef.astype(jnp.float32), slots_dev).astype(

time: 239 us -> 253 us (1.059)
  waiting for transfers between devices: 24.7 us -> 50.6 us
  blocking collectives: 79.9 us -> 64.3 us
    ppermute x0 -> x7, waiting for transfers between devices: none -> 25.9 us  [around_the_ring(): lax.ppermute(block, name, [(i, (i + 1) % n_dev) for i in range(n_dev)])]
    all_gather x1 -> x0, blocking collectives: 16.8 us -> none  [shards(): all_coef = lax.all_gather(coef, 'dp', axis=0, tiled=True)]
  transfers between devices with their start and end apart: 4 -> 11, of which waited for: 1 -> 6; matrix products, arithmetic and copies ran while one was open for 16% -> 16% of each run, Pallas kernels for 0% -> 0%
where the time goes in v1:
time: 253 us; the launch traced here: 252 us
  blocking collectives  64.3 us (25%)
  other arithmetic  62.4 us (25%)
  waiting for transfers between devices  50.6 us (20%)
  local copies, waits for them, and re-layouts  32.6 us (13%)
  matrix products  22.2 us (9%)
  between operations  14.6 us (6%)
  starting transfers between devices  5.68 us (2%)
    reduce_sum x2, other arithmetic, slot_table(): return jnp.sum(jnp.where(match, values_rows[:, :, None], 0.0), axis=1)  37.6 us
    unnamed x1, blocking collectives  26.9 us
    ppermute x7, waiting for transfers between devices, around_the_ring(): lax.ppermute(block, name, [(i, (i + 1) % n_dev) for i in range(n_dev)])  25.9 us
    reduce_scatter x1, waiting for transfers between devices, shards(): lax.psum_scatter(grad_part, 'leaf', scatter_dimension=0, tiled=True)  24.7 us
    all_gather x1, blocking collectives, shards(): all_slot = lax.all_gather(local_slot, 'dp', axis=0, tiled=True)  17.5 us
    mul x2, local copies, waits for them, and re-layouts, shards(): (emb_grad / P_SIZE)[:, None, :] * slope  15.2 us
    dot_general x1, matrix products, shards(): jnp.dot(features, head_weight, preferred_element_type=jnp.float32)  11.9 us
    all_gather x1, blocking collectives, shards(): grouped = lax.all_gather(embedded, 'leaf', axis=0, tiled=True)  10.2 us
  transfers between devices with their start and end apart: 11, of which 6 were waited for; matrix products, arithmetic and copies ran while one was open for 16% of the time, Pallas kernels for 0%

profile of v1, /device:TPU:0, one launch (start us, length us, event | category | flops | bytes accessed | tf_op | source)
XLA Modules:
  0.0 252.2 jit_solution(6073692515959603875)
XLA Ops:
  7.2 0.0 copy-start
  7.2 0.0 reduce-scatter.3.cloned.1.call-start
  7.2 0.9 add_select_fusion.3
  8.2 11.9 %fusion.1 = (f32[1600,1536]{1,0:T(8,128)}, f32[1600,1536]{1,0:T(8,128)}) fusion(f32[1536]{0:T(1024)} %param.10, f32[1536]{0:T(1024)} %param.9, bf16[1600,384]{1,0:T(8,128)(2,1)} %param.7, bf16[384,1536]{1,0:T(8,128)(2,1)} %param.8), kind=kOutput, calls=%fused_computation.11 | convolution fusion | flops 1902182400 | bytes 22081536 | tf_op jit(solution)/shard_map/dot_general | solution.py:30
  20.1 10.0 %reshape.27 = f32[16,100,1536]{2,1,0:T(8,128)} reshape(f32[1600,1536]{1,0:T(8,128)} %get-tuple-element.15) | data formatting | bytes 19660800 | tf_op jit(solution)/shard_map/reshape | solution.py:34
  30.1 5.3 %reduce_sum.74 = f32[16,1536]{1,0:T(8,128)S(1)} reduce(f32[16,100,1536]{2,1,0:T(8,128)} %reshape.27, f32[]{:T(128)} %constant.87.clone.1), dimensions={1}, to_apply=%region_2.3 | reduce | flops 2433024 | bytes 9928708 | tf_op jit(solution)/shard_map/reduce_sum | solution.py:34
  35.5 10.2 %all_gather.6 = bf16[64,1536]{1,0:T(8,128)(2,1)S(1)} all-gather(bf16[16,1536]{1,0:T(8,128)(2,1)S(1)} %multiply_convert_fusion.4), channel_id=1, replica_groups=mesh['dp'=8,'leaf'=4] {'leaf'}, dimensions={0}, use_global_device_ids=true | all-gather | bytes 245760 | tf_op jit(solution)/shard_map/all_gather | solution.py:35
  45.6 1.8 select_reduce_fusion.4
  47.5 0.1 fusion.15
  47.6 9.4 %select_reduce_fusion.3 = (f32[64,1024]{1,0:T(8,128)S(1)}, f32[64,1024]{1,0:T(8,128)S(1)}) fusion(s32[64,64]{1,0:T(8,128)S(1)} %get-tuple-element.13, pred[64,64]{1,0:T(8,128)(4,1)S(1)} %get-tuple-element.14, f32[64]{0:T(128)S(1)} %compare_convert_fusion), kind=kLoop, calls=%fused_computation.4 | loop fusion | flops 25034752 | bytes 545024 | tf_op jit(solution)/shard_map/reduce_sum | solution.py:24
  56.9 1.8 fusion.21
  58.7 1.4 fusion.22
  60.1 0.0 reduce-scatter.3.cloned.1.call-update
  60.2 0.2 reduce-scatter.5.cloned.1.call-start
  60.4 24.7 %reduce-scatter.3.cloned.1.call-done = f32[16,1536]{1,0:T(8,128)} async-done(((f32[64,1536]{1,0:T(8,128)}), f32[16,1536]{1,0:T(8,128)}) %reduce-scatter.3.cloned.1.call-update) | async-done | bytes 98320 | tf_op jit(solution)/shard_map/reduce_scatter | solution.py:57
  85.1 0.9 broadcast_multiply_fusion
  86.0 5.2 %mul.48 = f32[16,100,1536]{2,1,0:T(8,128)} broadcast(f32[16,1536]{1,0:T(8,128)S(1)} %broadcast_multiply_fusion), dimensions={0,2} | broadcast | bytes 9928704 | tf_op jit(solution)/shard_map/mul | solution.py:74
  91.2 10.0 %mul.49 = f32[1600,1536]{1,0:T(8,128)} reshape(f32[16,100,1536]{2,1,0:T(8,128)} %mul.48) | data formatting | bytes 19660800 | tf_op jit(solution)/shard_map/mul | solution.py:74
  101.2 9.6 %fusion.20 = (f32[1536]{0:T(1024)}, f32[1536]{0:T(1024)}, f32[1600,1536]{1,0:T(8,128)S(1)}) fusion(f32[1600,1536]{1,0:T(8,128)} %get-tuple-element.16, f32[1600,1536]{1,0:T(8,128)} %mul.49, f32[1536]{0:T(1024)S(1)} %copy-done.2, f32[1536]{0:T(1024)S(1)} %copy-done.3), kind=kLoop, calls=%fused_computation.69 | loop fusion | flops 31945728 | bytes 29515776 | tf_op jit(solution)/shard_map/reduce_sum | solution.py:80
  110.8 4.5 %fusion.4 = f32[384,1536]{0,1:T(8,128)} fusion(bf16[1600,384]{1,0:T(8,128)(2,1)S(1)} %copy-done.5, f32[1600,1536]{1,0:T(8,128)S(1)} %get-tuple-element.12, f32[1536]{0:T(1024)S(1)} %copy-done.3), kind=kOutput, calls=%fused_computation.15 | convolution fusion | flops 1892352000 | bytes 13424640 | tf_op jit(solution)/shard_map/dot_general | solution.py:76
  115.3 0.0 reduce-scatter.5.cloned.1.call-update
  115.3 5.3 %select_reduce_fusion.1 = bf16[64,64]{1,0:T(8,128)(2,1)S(1)} fusion(f32[64,1024]{1,0:T(8,128)} %get-tuple-element.17, s32[64,64]{1,0:T(8,128)S(1)} %get-tuple-element.13, pred[64,64]{1,0:T(8,128)(4,1)S(1)} %get-tuple-element.14), kind=kLoop, calls=%fused_computation.2 | loop fusion | flops 16773120 | bytes 290816 | tf_op jit(solution)/shard_map/reduce_sum | solution.py:60
  120.7 0.0 collective-permute-start
  120.7 5.1 %collective-permute-done = bf16[64,64]{1,0:T(8,128)(2,1)S(1)} collective-permute-done((bf16[64,64]{1,0:T(8,128)(2,1)S(1)}, bf16[64,64]{1,0:T(8,128)(2,1)S(1)}, u32[]{:S(2)}, u32[]{:S(2)}) %collective-permute-start) | collective-permute-done | bytes 8224 | tf_op jit(solution)/shard_map/ppermute | solution.py:15
  125.8 0.0 collective-permute-start.1
  125.8 5.3 %collective-permute-done.1 = bf16[64,64]{1,0:T(8,128)(2,1)S(1)} collective-permute-done((bf16[64,64]{1,0:T(8,128)(2,1)S(1)}, bf16[64,64]{1,0:T(8,128)(2,1)S(1)}, u32[]{:S(2)}, u32[]{:S(2)}) %collective-permute-start.1) | collective-permute-done | bytes 8224 | tf_op jit(solution)/shard_map/ppermute | solution.py:15
  131.1 5.1 %collective-permute-done.2 = bf16[64,64]{1,0:T(8,128)(2,1)S(1)} collective-permute-done((bf16[64,64]{1,0:T(8,128)(2,1)S(1)}, bf16[64,64]{1,0:T(8,128)(2,1)S(1)}, u32[]{:S(2)}, u32[]{:S(2)}) %collective-permute-start.2) | collective-permute-done | bytes 8224 | tf_op jit(solution)/shard_map/ppermute | solution.py:15
  136.3 5.1 %collective-permute-done.3 = bf16[64,64]{1,0:T(8,128)(2,1)S(1)} collective-permute-done((bf16[64,64]{1,0:T(8,128)(2,1)S(1)}, bf16[64,64]{1,0:T(8,128)(2,1)S(1)}, u32[]{:S(2)}, u32[]{:S(2)}) %collective-permute-start.3) | collective-permute-done | bytes 8224 | tf_op jit(solution)/shard_map/ppermute | solution.py:15
  141.4 0.0 collective-permute-start.4
  141.4 5.2 %collective-permute-done.4 = bf16[64,64]{1,0:T(8,128)(2,1)S(1)} collective-permute-done((bf16[64,64]{1,0:T(8,128)(2,1)S(1)}, bf16[64,64]{1,0:T(8,128)(2,1)S(1)}, u32[]{:S(2)}, u32[]{:S(2)}) %collective-permute-start.4) | collective-permute-done | bytes 8224 | tf_op jit(solution)/shard_map/ppermute | solution.py:15
  146.6 0.9 all_to_all.14
  147.5 1.7 copy.13
  149.2 4.8 %all-to-all-start = ((bf16[64,8,192]{2,0,1:T(8,128)(2,1)}), bf16[64,8,192]{2,0,1:T(8,128)(2,1)}, u32[]{:S(2)}, u32[]{:S(2)}) async-start(bf16[64,8,192]{2,0,1:T(8,128)(2,1)} %copy.13), calls=%async_computation.2 | async-start | bytes 524288 | tf_op jit(solution)/shard_map/all_to_all | solution.py:63
  154.1 0.0 all-reduce.6.cloned.1.call-start
  154.1 0.5 collective-permute-start.6
  154.6 17.5 %all_gather.7 = s32[512,64]{1,0:T(8,128)S(1)} all-gather(s32[64,64]{1,0:T(8,128)S(1)} %get-tuple-element.13), channel_id=1, replica_groups=mesh['dp'=8,'leaf'=4] {'dp'}, dimensions={0}, use_global_device_ids=true | all-gather | bytes 147456 | tf_op jit(solution)/shard_map/all_gather | solution.py:65
  172.1 1.2 dynamic-slice
  174.0 0.7 constant_dynamic-update-slice_fusion.15
  174.8 0.7 constant_dynamic-update-slice_fusion.7
  175.6 0.7 dynamic-slice_convert_fusion
  176.3 0.0 all-reduce.6.cloned.1.call-update
  176.4 28.3 %select_reduce_fusion = bf16[512,1024]{1,0:T(8,128)(2,1)} fusion(f32[512,64]{1,0:T(8,128)} %dynamic-slice_convert_fusion, s32[512,64]{1,0:T(8,128)S(1)} %all_gather.7), kind=kLoop, calls=%fused_computation | loop fusion | flops 100139008 | bytes 1310720 | tf_op jit(solution)/shard_map/reduce_sum | solution.py:24
  204.6 2.6 %fusion.23 = f32[1024,192]{0,1:T(8,128)} fusion(bf16[512,1024]{1,0:T(8,128)(2,1)} %select_reduce_fusion, bf16[512,192]{1,0:T(8,128)(2,1)} %bitcast.2), kind=kOutput, calls=%fused_computation.72 | convolution fusion | flops 201326592 | bytes 2031616 | tf_op jit(solution)/shard_map/dot_general | solution.py:70
  207.2 26.9 %all-reduce.2 = (f32[1536]{0:T(1024)S(1)}, f32[1536]{0:T(1024)S(1)}) all-reduce(f32[1536]{0:T(1024)} %get-tuple-element.5, f32[1536]{0:T(1024)} %get-tuple-element.4), channel_id=4, replica_groups=mesh['dp'=8,'leaf'=4] {'dp'}, use_global_device_ids=true, to_apply=%region_8.9.clone | all-reduce | flops 3072 | bytes 24576
  234.1 0.1 dynamic-slice.1
  234.1 0.1 dynamic-slice.3
  234.2 9.8 %all-reduce.3 = (f32[192]{0:T(256)}, f32[192]{0:T(256)}) all-reduce(f32[192]{0:T(256)S(1)} %dynamic-slice.1, f32[192]{0:T(256)S(1)} %dynamic-slice.3), channel_id=1, replica_groups=mesh['dp'=8,'leaf'=4] {'leaf'}, use_global_device_ids=true, to_apply=%region_9.10 | all-reduce | flops 384 | bytes 3072 | tf_op jit(solution)/shard_map/psum | solution.py:86
  244.0 1.7 copy.30
  (35 shorter events, 0.2 us)
Async XLA Ops:
  7.2 49.8 %copy-start = (bf16[1024,1536]{1,0:T(8,128)(2,1)S(1)}, bf16[1024,1536]{1,0:T(8,128)(2,1)}, u32[]{:S(2)}) copy-start(bf16[1024,1536]{1,0:T(8,128)(2,1)} %param.11) | copy-start | bytes 9437188
  7.2 77.9 %reduce-scatter.3.cloned.1.call-start = ((), (), s32[]{:S(2)}) async-start(), calls=%async_computation.3 | async-start | bytes 491520 | tf_op jit(solution)/shard_map/reduce_scatter | solution.py:57
  30.1 15.5 %copy-start.4 = (s32[64]{0:T(128)S(1)}, s32[64]{0:T(128)}, u32[]{:S(2)}) copy-start(s32[64]{0:T(128)} %param.12) | copy-start | bytes 772
  30.1 17.3 %copy-start.1 = (s32[64,64]{1,0:T(8,128)S(1)}, s32[64,64]{1,0:T(8,128)}, u32[]{:S(2)}) copy-start(s32[64,64]{1,0:T(8,128)} %param.13) | copy-start | bytes 49156
  60.2 116.2 %reduce-scatter.5.cloned.1.call-start = ((), (), s32[]{:S(2)}) async-start(), calls=%async_computation.4 | async-start | bytes 2654208 | tf_op jit(solution)/shard_map/reduce_scatter | solution.py:82
  91.1 10.1 %copy-start.2 = (f32[1536]{0:T(1024)S(1)}, f32[1536]{0:T(1024)}, u32[]{:S(2)}) copy-start(f32[1536]{0:T(1024)} %param.10) | copy-start | bytes 18436
  91.2 10.1 %copy-start.3 = (f32[1536]{0:T(1024)S(1)}, f32[1536]{0:T(1024)}, u32[]{:S(2)}) copy-start(f32[1536]{0:T(1024)} %param.9) | copy-start | bytes 18436
  101.2 9.6 %copy-start.5 = (bf16[1600,384]{1,0:T(8,128)(2,1)S(1)}, bf16[1600,384]{1,0:T(8,128)(2,1)}, u32[]{:S(2)}) copy-start(bf16[1600,384]{1,0:T(8,128)(2,1)} %param.7) | copy-start | bytes 3686404
  120.7 5.1 %collective-permute-start = (bf16[64,64]{1,0:T(8,128)(2,1)S(1)}, bf16[64,64]{1,0:T(8,128)(2,1)S(1)}, u32[]{:S(2)}, u32[]{:S(2)}) collective-permute-start(bf16[64,64]{1,0:T(8,128)(2,1)S(1)} %select_reduce_fusion.1), channel_id=1, source_target_pairs={{0,4},{4,8},{8,12},{12,16},{16,20},{20,24},{24,28},{28,0},{1,5},{5... | collective-permute-start | bytes 24584 | tf_op jit(solution)/shard_map/ppermute | solution.py:15
  125.8 5.3 %collective-permute-start.1 = (bf16[64,64]{1,0:T(8,128)(2,1)S(1)}, bf16[64,64]{1,0:T(8,128)(2,1)S(1)}, u32[]{:S(2)}, u32[]{:S(2)}) collective-permute-start(bf16[64,64]{1,0:T(8,128)(2,1)S(1)} %collective-permute-done), channel_id=1, source_target_pairs={{0,4},{4,8},{8,12},{12,16},{16,20},{20,24},{24,28},{28,0},{1,5},{5... | collective-permute-start | bytes 24584 | tf_op jit(solution)/shard_map/ppermute | solution.py:15
  131.1 5.1 %collective-permute-start.2 = (bf16[64,64]{1,0:T(8,128)(2,1)S(1)}, bf16[64,64]{1,0:T(8,128)(2,1)S(1)}, u32[]{:S(2)}, u32[]{:S(2)}) collective-permute-start(bf16[64,64]{1,0:T(8,128)(2,1)S(1)} %collective-permute-done.1), channel_id=1, source_target_pairs={{0,4},{4,8},{8,12},{12,16},{16,20},{20,24},{24,28},{28,0},{1,5},{5... | collective-permute-start | bytes 24584 | tf_op jit(solution)/shard_map/ppermute | solution.py:15
  136.3 5.1 %collective-permute-start.3 = (bf16[64,64]{1,0:T(8,128)(2,1)S(1)}, bf16[64,64]{1,0:T(8,128)(2,1)S(1)}, u32[]{:S(2)}, u32[]{:S(2)}) collective-permute-start(bf16[64,64]{1,0:T(8,128)(2,1)S(1)} %collective-permute-done.2), channel_id=1, source_target_pairs={{0,4},{4,8},{8,12},{12,16},{16,20},{20,24},{24,28},{28,0},{1,5},{5... | collective-permute-start | bytes 24584 | tf_op jit(solution)/shard_map/ppermute | solution.py:15
  141.4 5.2 %collective-permute-start.4 = (bf16[64,64]{1,0:T(8,128)(2,1)S(1)}, bf16[64,64]{1,0:T(8,128)(2,1)S(1)}, u32[]{:S(2)}, u32[]{:S(2)}) collective-permute-start(bf16[64,64]{1,0:T(8,128)(2,1)S(1)} %collective-permute-done.3), channel_id=1, source_target_pairs={{0,4},{4,8},{8,12},{12,16},{16,20},{20,24},{24,28},{28,0},{1,5},{5... | collective-permute-start | bytes 24584 | tf_op jit(solution)/shard_map/ppermute | solution.py:15
  146.6 7.5 %collective-permute-start.5 = (bf16[64,64]{1,0:T(8,128)(2,1)S(1)}, bf16[64,64]{1,0:T(8,128)(2,1)S(1)}, u32[]{:S(2)}, u32[]{:S(2)}) collective-permute-start(bf16[64,64]{1,0:T(8,128)(2,1)S(1)} %collective-permute-done.4), channel_id=1, source_target_pairs={{0,4},{4,8},{8,12},{12,16},{16,20},{20,24},{24,28},{28,0},{1,5},{5... | collective-permute-start | bytes 24584 | tf_op jit(solution)/shard_map/ppermute | solution.py:15
  149.2 55.4 %all-to-all-start = ((bf16[64,8,192]{2,0,1:T(8,128)(2,1)}), bf16[64,8,192]{2,0,1:T(8,128)(2,1)}, u32[]{:S(2)}, u32[]{:S(2)}) async-start(bf16[64,8,192]{2,0,1:T(8,128)(2,1)} %copy.13), calls=%async_computation.2 | async-start | bytes 524288 | tf_op jit(solution)/shard_map/all_to_all | solution.py:63
  154.1 89.9 %all-reduce.6.cloned.1.call-start = ((), (), s32[]{:S(2)}) async-start(), calls=%async_computation.5 | async-start | bytes 589824 | tf_op jit(solution)/shard_map/psum | solution.py:86
  154.1 19.9 %collective-permute-start.6 = (bf16[64,64]{1,0:T(8,128)(2,1)S(1)}, bf16[64,64]{1,0:T(8,128)(2,1)}, u32[]{:S(2)}, u32[]{:S(2)}) collective-permute-start(bf16[64,64]{1,0:T(8,128)(2,1)S(1)} %collective-permute-done.5), channel_id=1, source_target_pairs={{0,4},{4,8},{8,12},{12,16},{16,20},{20,24},{24,28},{28,0},{1,5},{5... | collective-permute-start | bytes 24584 | tf_op jit(solution)/shard_map/ppermute | solution.py:15
Sparse Core Ops, SparseCore 0:
  60.3 24.7 reduce-scatter.2
  115.5 37.1 reduce-scatter.4
  176.5 41.4 all-reduce.5
